TPU v7x, 256 devices: a whole 4x4x8 slice. The times are simulated.
256 devices in a mesh: ctx: 16 (over z, core), ch: 16 (over y, x).
Axes of the slice: x: 4, y: 4, z: 8, core: 2. Of those that a mesh axis runs over, the one named last changes fastest.
Arguments:
- inputs: bfloat16 [4096, 4096], P('ctx', 'ch'), may hold values from -6 to 6
- gating: bfloat16 [4096, 4096], P('ctx', 'ch'), may hold values from -6 to 6
- filter_taps: bfloat16 [4096, 4096], P('ctx', 'ch'), may hold values from -2.25 to 2.25
- skip_gain: float32 [4096], P('ch'), may hold values from 0.5 to 1.5
- w_out: bfloat16 [4096, 4096], P('ch'), may hold values from -0.09375 to 0.09375
- cotangent: bfloat16 [4096, 4096], P('ctx', 'ch'), may hold values from -0.3125 to 0.3125
Outputs:
- output: bfloat16 [4096, 4096], P('ctx', 'ch')
- filter_grad: float32 [4096, 4096], P('ctx', 'ch')
All inputs are finite; a program needn't handle non-finite values.
Results may differ from a plain program's by a relative error of at most 0.015.
Values may be sent and summed in bfloat16 or wider, within the bound.
No kernel may reach another device: no remote copies, remote signals or barrier semaphores. Data moves between devices by JAX's collectives and lax.ppermute only.
A program may use at most 64 MiB of HBM per device.

v0:
```python
import math
import jax
import jax.numpy as jnp
from jax import lax
from jax.sharding import PartitionSpec as P

exact_prec = lax.Precision.HIGHEST


def spectral_tables(block_len):
    time_ids = jnp.arange(2 * block_len, dtype=jnp.int32)
    freq_ids = jnp.arange(block_len, dtype=jnp.int32)
    phase_ids = freq_ids[:, None] * time_ids[None, :] % (2 * block_len)
    angles = phase_ids.astype(jnp.float32) * (math.pi / block_len)
    parity = jnp.where(time_ids % 2 == 0, 1.0, -1.0).astype(jnp.float32)[None, :]
    is_first = (freq_ids == 0)[:, None]
    forward = jnp.concatenate(
        [jnp.cos(angles), jnp.where(is_first, parity, -jnp.sin(angles))], axis=0
    )
    norm_scale = 1.0 / (2 * block_len)
    real_rows = jnp.where(is_first, 1.0, 2.0) * jnp.cos(angles) * norm_scale
    imag_rows = jnp.where(is_first, parity, -2.0 * jnp.sin(angles)) * norm_scale
    inverse = jnp.concatenate([real_rows, imag_rows], axis=0).T
    first_bin = is_first.astype(jnp.float32)
    return (forward, inverse, first_bin)


def spec_product(first_spec, second_spec, first_bin):
    bin_count = first_bin.shape[0]
    first_real, first_imag = (first_spec[..., :bin_count, :], first_spec[..., bin_count:, :])
    second_real, second_imag = (second_spec[..., :bin_count, :], second_spec[..., bin_count:, :])
    others = 1.0 - first_bin
    real_part = first_real * second_real - others * first_imag * second_imag
    imag_part = (
        others * (first_real * second_imag + first_imag * second_real)
        + first_bin * first_imag * second_imag
    )
    return jnp.concatenate([real_part, imag_part], axis=-2)


def conj_product(first_spec, second_spec, first_bin):
    bin_count = first_bin.shape[0]
    first_real, first_imag = (first_spec[..., :bin_count, :], first_spec[..., bin_count:, :])
    second_real, second_imag = (second_spec[..., :bin_count, :], second_spec[..., bin_count:, :])
    others = 1.0 - first_bin
    real_part = first_real * second_real + others * first_imag * second_imag
    imag_part = (
        others * (first_imag * second_real - first_real * second_imag)
        + first_bin * first_imag * second_imag
    )
    return jnp.concatenate([real_part, imag_part], axis=-2)


def transform(dft_table, block_rows):
    return jnp.dot(dft_table, block_rows.astype(jnp.float32), precision=exact_prec)


def shift_blocks(spec, blocks, width):
    if blocks == 0:
        return spec
    rows = spec.shape[0]
    pad = jnp.zeros((rows, blocks * width), spec.dtype)
    return jnp.concatenate([pad, spec[:, : spec.shape[1] - blocks * width]], axis=1)


def body(inputs, gating, filter_taps, skip_gain, w_out, cotangent):
    block_len, channels = inputs.shape
    ctx_count = lax.axis_size("ctx")
    width = channels // ctx_count
    forward, inverse, first_bin = spectral_tables(block_len)
    first_half = forward[:, :block_len]
    second_half = forward[:, block_len:]
    pair = jnp.stack([inputs, filter_taps])
    pair_t = lax.all_to_all(pair, "ctx", 2, 2, tiled=True)
    signal_t, taps_t = (pair_t[0], pair_t[1])
    upstream = lax.dot_general(
        lax.all_gather(cotangent, "ch", axis=1, tiled=True),
        w_out,
        (((1,), (1,)), ((), ())),
        preferred_element_type=jnp.float32,
    )
    gate_wide = gating.astype(jnp.float32)
    grad_mixed = upstream * gate_wide
    grad_t = lax.all_to_all(grad_mixed, "ctx", 1, 1, tiled=True)
    low_spec = transform(first_half, signal_t)
    high_spec = transform(second_half, signal_t)
    seg_spec = high_spec + shift_blocks(low_spec, 1, width)
    taps_spec = transform(first_half, taps_t)
    grad_spec = transform(second_half, grad_t)
    running = jnp.zeros_like(seg_spec)
    lag_terms = []
    for lag in range(ctx_count):
        shifted = shift_blocks(seg_spec, lag, width)
        tap_block = taps_spec[:, lag * width : (lag + 1) * width]
        running = running + spec_product(jnp.tile(tap_block, (1, ctx_count)), shifted, first_bin)
        term = conj_product(grad_spec, shifted, first_bin)
        lag_terms.append(term.reshape(term.shape[0], ctx_count, width).sum(axis=1))
    lag_spec = jnp.concatenate(lag_terms, axis=1)
    convolved_t = jnp.dot(inverse[block_len:], running, precision=exact_prec)
    filter_grad_t = jnp.dot(inverse[:block_len], lag_spec, precision=exact_prec)
    back = lax.all_to_all(jnp.stack([convolved_t, filter_grad_t]), "ctx", 2, 2, tiled=True)
    convolved, filter_grad = (back[0], back[1])
    mixed_sum = convolved + skip_gain[None, :] * inputs.astype(jnp.float32)
    gated_rows = (gate_wide * mixed_sum).astype(jnp.bfloat16)
    partial_out = jnp.dot(gated_rows, w_out, preferred_element_type=jnp.float32)
    output = lax.psum_scatter(
        partial_out.astype(jnp.bfloat16), "ch", scatter_dimension=1, tiled=True
    )
    return (output, filter_grad)


def solution(mesh):
    return jax.shard_map(
        body,
        mesh=mesh,
        in_specs=(
            P("ctx", "ch"),
            P("ctx", "ch"),
            P("ctx", "ch"),
            P("ch"),
            P("ch", None),
            P("ctx", "ch"),
        ),
        out_specs=(P("ctx", "ch"), P("ctx", "ch")),
        check_vma=False,
    )
```

profile of v0, /device:TPU:2, one launch (start us, length us, event | category | flops | bytes accessed | tf_op | source)
XLA Modules:
  0.0 263.9 jit_solution(2376567963497250367)
XLA Ops:
  9.8 8.6 %all-to-all-start = ((bf16[2,256,256]{1,0,2:T(2,128)(2,1)}), bf16[2,256,256]{1,0,2:T(2,128)(2,1)S(1)}, u32[]{:S(2)}, u32[]{:S(2)}) async-start(bf16[2,256,256]{1,0,2:T(2,128)(2,1)} %copy.25), calls=%async_computation | async-start | bytes 524288 | tf_op jit(solution)/shard_map/all_to_all | solution.py:74
  19.4 1.9 fusion.170
  21.3 2.0 multiply_multiply_fusion
  23.3 2.0 select_multiply_fusion
  26.5 3.0 %all-to-all-done = bf16[2,256,256]{1,0,2:T(2,128)(2,1)S(1)} async-done(((bf16[2,256,256]{1,0,2:T(2,128)(2,1)}), bf16[2,256,256]{1,0,2:T(2,128)(2,1)S(1)}, u32[]{:S(2)}, u32[]{:S(2)}) %all-to-all-start) | async-done | bytes 262176 | tf_op jit(solution)/shard_map/all_to_all | solution.py:74
  35.3 29.8 %all-gather.2.cloned.1.call-done = bf16[256,4096]{1,0:T(8,128)(2,1)} async-done(((bf16[256,256]{1,0:T(8,128)(2,1)}), bf16[256,4096]{1,0:T(8,128)(2,1)}) %all-gather.2.cloned.1.call-update) | async-done | bytes 2097168 | tf_op jit(solution)/shard_map/all_gather | solution.py:77
  65.1 3.0 %convolution_multiply_fusion = f32[256,256]{0,1:T(8,128)} fusion(bf16[256,4096]{1,0:T(8,128)(2,1)} %all-gather.2.cloned.1.call-done, bf16[256,4096]{1,0:T(8,128)(2,1)S(1)} %copy-done, bf16[256,256]{0,1:T(8,128)(2,1)S(1)} %copy.24), kind=kOutput, calls=%fused_computation.4 | convolution fusion | flops 537001984 | bytes 4587520 | tf_op jit(solution)/shard_map/dot_general | solution.py:76
  68.1 7.1 %all-to-all-start.1 = ((f32[256,16,16]{0,2,1:T(8,128)}), f32[256,16,16]{0,2,1:T(8,128)S(1)}, u32[]{:S(2)}, u32[]{:S(2)}) async-start(f32[256,16,16]{0,2,1:T(8,128)} %bitcast.38), calls=%async_computation.1 | async-start | bytes 524288 | tf_op jit(solution)/shard_map/all_to_all | solution.py:84
  82.2 4.2 %all-to-all-done.1 = f32[256,16,16]{0,2,1:T(8,128)S(1)} async-done(((f32[256,16,16]{0,2,1:T(8,128)}), f32[256,16,16]{0,2,1:T(8,128)S(1)}, u32[]{:S(2)}, u32[]{:S(2)}) %all-to-all-start.1) | async-done | bytes 262176 | tf_op jit(solution)/shard_map/all_to_all | solution.py:84
  86.4 1.7 fusion.171
  88.1 1.7 fusion.72
  90.5 2.7 %fusion.76 = (f32[256,256]{0,1:T(8,128)}, f32[256,256]{0,1:T(8,128)}, f32[256,256]{0,1:T(8,128)S(1)}, f32[256,256]{0,1:T(8,128)S(1)}, f32[256,256]{0,1:T(8,128)S(1)}, /*index=5*/f32[256,256]{0,1:T(8,128)S(1)}) fusion(f32[256,16]{0,1:T(8,128)S(1)} %copy-done.40, f32[256,16]{0,1:T(8,128)S(1)} %copy-done.41, f32[256]{0:T(256)S(1)} %broadcast_subtract_fusion, ...), kind=kLoop, calls=%fused_computation.219 | loop fusion | flops 2031616 | bytes 2656256 | tf_op jit(solution)/shard_map/sub | solution.py:33
  94.4 1.7 reduce_sum.145
  96.1 1.7 reduce_sum.159
  99.7 1.7 reduce_sum.147
  102.0 2.0 fusion.88
  105.2 1.7 reduce_sum.148
  110.0 1.7 reduce_sum.146
  112.3 2.1 fusion.92
  115.4 1.7 reduce_sum.149
  117.7 1.9 fusion.132
  120.5 1.7 reduce_sum.152
  124.1 1.7 reduce_sum.151
  126.4 2.1 fusion.96
  129.6 1.7 reduce_sum.150
  131.3 1.7 reduce_sum.154
  150.5 2.0 convolution_bitcast_fusion
  152.6 4.2 %convolution_bitcast_fusion.1 = f32[1,256,256]{2,1,0:T(8,128)S(1)} fusion(f32[512,512]{0,1:T(8,128)S(1)} %copy-done.4, f32[256,256]{0,1:T(8,128)} %get-tuple-element.37, f32[256,256]{0,1:T(8,128)S(1)} %copy-done.21, f32[256,256]{0,1:T(8,128)} %get-tuple-element.57, f32[256,256]{0,1:T(8,128)} %get-tuple-element.56, f32[256,256]{0,1:T(8,128)} %get-tuple-element.97, ...), kind=kOutput, calls=%fused_computation.3 | convolution fusion | flops 406716416 | bytes 9175040 | tf_op jit(solution)/shard_map/dot_general | solution.py:99
  157.9 3.6 %all-to-all-start.2 = ((f32[2,256,256]{1,0,2:T(2,128)}), f32[2,256,256]{1,0,2:T(2,128)S(1)}, u32[]{:S(2)}, u32[]{:S(2)}) async-start(f32[2,256,256]{1,0,2:T(2,128)} %copy.30), calls=%async_computation.2 | async-start | bytes 1048576 | tf_op jit(solution)/shard_map/all_to_all | solution.py:101
  161.6 15.8 %all-to-all-done.2 = f32[2,256,256]{1,0,2:T(2,128)S(1)} async-done(((f32[2,256,256]{1,0,2:T(2,128)}), f32[2,256,256]{1,0,2:T(2,128)S(1)}, u32[]{:S(2)}, u32[]{:S(2)}) %all-to-all-start.2) | async-done | bytes 524320 | tf_op jit(solution)/shard_map/all_to_all | solution.py:101
  177.9 2.2 convolution_convert_fusion
  180.9 76.1 %reduce-scatter.2.cloned.1.call-done = bf16[256,256]{1,0:T(8,128)(2,1)} async-done(((bf16[256,4096]{1,0:T(8,128)(2,1)}), bf16[256,256]{1,0:T(8,128)(2,1)}) %reduce-scatter.2.cloned.1.call-update) | async-done | bytes 131088 | tf_op jit(solution)/shard_map/reduce_scatter | solution.py:106
  (170 shorter events, 52.8 us)
Async XLA Ops:
  7.2 57.9 %copy-start = (bf16[256,4096]{1,0:T(8,128)(2,1)S(1)}, bf16[256,4096]{1,0:T(8,128)(2,1)}, u32[]{:S(2)}) copy-start(bf16[256,4096]{1,0:T(8,128)(2,1)} %param.10) | copy-start | bytes 6291460
  7.2 57.9 %all-gather.2.cloned.1.call-start = ((), (), s32[]{:S(2)}) async-start(), calls=%async_computation.4 | async-start | bytes 2228224 | tf_op jit(solution)/shard_map/all_gather | solution.py:77
  9.8 19.7 %all-to-all-start = ((bf16[2,256,256]{1,0,2:T(2,128)(2,1)}), bf16[2,256,256]{1,0,2:T(2,128)(2,1)S(1)}, u32[]{:S(2)}, u32[]{:S(2)}) async-start(bf16[2,256,256]{1,0,2:T(2,128)(2,1)} %copy.25), calls=%async_computation | async-start | bytes 524288 | tf_op jit(solution)/shard_map/all_to_all | solution.py:74
  19.4 45.7 %copy-start.10 = (bf16[256,256]{0,1:T(8,128)(2,1)}, bf16[256,256]{0,1:T(8,128)(2,1)S(1)}, u32[]{:S(2)}) copy-start(bf16[256,256]{0,1:T(8,128)(2,1)S(1)} %copy.24) | copy-start | bytes 393220
  21.3 53.9 %copy-start.2 = (f32[256,512]{1,0:T(8,128)}, f32[256,512]{1,0:T(8,128)S(1)}, u32[]{:S(2)}) copy-start(f32[256,512]{1,0:T(8,128)S(1)} %fusion.170) | copy-start | bytes 1572868
  25.4 8.7 %copy-start.3 = (f32[256,512]{1,0:T(8,128)}, f32[256,512]{1,0:T(8,128)S(1)}, u32[]{:S(2)}) copy-start(f32[256,512]{1,0:T(8,128)S(1)} %get-tuple-element.153) | copy-start | bytes 1572868
  68.1 18.3 %all-to-all-start.1 = ((f32[256,16,16]{0,2,1:T(8,128)}), f32[256,16,16]{0,2,1:T(8,128)S(1)}, u32[]{:S(2)}, u32[]{:S(2)}) async-start(f32[256,16,16]{0,2,1:T(8,128)} %bitcast.38), calls=%async_computation.1 | async-start | bytes 524288 | tf_op jit(solution)/shard_map/all_to_all | solution.py:84
  76.8 11.2 %copy-start.1 = (f32[512,256]{0,1:T(8,128)}, f32[512,256]{0,1:T(8,128)S(1)}, u32[]{:S(2)}) copy-start(f32[512,256]{0,1:T(8,128)S(1)} %convolution_add_fusion) | copy-start | bytes 1572868
  76.9 13.7 %copy-start.25 = (f32[512,16]{0,1:T(8,128)}, f32[512,16]{0,1:T(8,128)S(1)}, u32[]{:S(2)}) copy-start(f32[512,16]{0,1:T(8,128)S(1)} %slice.604) | copy-start | bytes 98308
  93.2 4.5 %slice-start.5 = ((f32[512,256]{0,1:T(8,128)}), f32[512,208]{0,1:T(8,128)S(1)}, s32[]{:S(2)}) async-start(f32[512,256]{0,1:T(8,128)} %copy-done.1), calls=%async_computation.11 | async-start | bytes 851968 | tf_op jit(solution)/shard_map/slice | solution.py:63
  93.2 4.5 %copy-start.38 = (f32[256,16]{0,1:T(8,128)S(1)}, f32[256,16]{0,1:T(8,128)}, u32[]{:S(2)}) copy-start(f32[256,16]{0,1:T(8,128)} %get-tuple-element.84) | copy-start | bytes 49156
  93.2 4.5 %copy-start.39 = (f32[256,16]{0,1:T(8,128)S(1)}, f32[256,16]{0,1:T(8,128)}, u32[]{:S(2)}) copy-start(f32[256,16]{0,1:T(8,128)} %get-tuple-element.85) | copy-start | bytes 49156
  117.7 4.5 %copy-start.31 = (f32[256,16]{0,1:T(8,128)S(1)}, f32[256,16]{0,1:T(8,128)}, u32[]{:S(2)}) copy-start(f32[256,16]{0,1:T(8,128)} %get-tuple-element.76) | copy-start | bytes 49156
  117.7 4.5 %copy-start.32 = (f32[256,16]{0,1:T(8,128)S(1)}, f32[256,16]{0,1:T(8,128)}, u32[]{:S(2)}) copy-start(f32[256,16]{0,1:T(8,128)} %get-tuple-element.77) | copy-start | bytes 49156
  128.5 4.5 %copy-start.29 = (f32[512,16]{0,1:T(8,128)S(1)}, f32[512,16]{0,1:T(8,128)}, u32[]{:S(2)}) copy-start(f32[512,16]{0,1:T(8,128)} %reduce_sum.145) | copy-start | bytes 98308
  128.5 19.4 %copy-start.28 = (f32[512,16]{0,1:T(8,128)S(1)}, f32[512,16]{0,1:T(8,128)}, u32[]{:S(2)}) copy-start(f32[512,16]{0,1:T(8,128)} %reduce_sum.157) | copy-start | bytes 98308
  128.5 21.4 %copy-start.27 = (f32[512,16]{0,1:T(8,128)S(1)}, f32[512,16]{0,1:T(8,128)}, u32[]{:S(2)}) copy-start(f32[512,16]{0,1:T(8,128)} %reduce_sum.159) | copy-start | bytes 98308
  128.5 22.0 %copy-start.4 = (f32[512,512]{0,1:T(8,128)S(1)}, f32[512,512]{0,1:T(8,128)}, u32[]{:S(2)}) copy-start(f32[512,512]{0,1:T(8,128)} %maximum_bitcast_fusion) | copy-start | bytes 3145732
  129.6 22.9 %copy-start.13 = (f32[256,256]{0,1:T(8,128)S(1)}, f32[256,256]{0,1:T(8,128)}, u32[]{:S(2)}) copy-start(f32[256,256]{0,1:T(8,128)} %get-tuple-element.148) | copy-start | bytes 786436
  133.0 19.5 %copy-start.14 = (f32[256,256]{0,1:T(8,128)S(1)}, f32[256,256]{0,1:T(8,128)}, u32[]{:S(2)}) copy-start(f32[256,256]{0,1:T(8,128)} %get-tuple-element.149) | copy-start | bytes 786436
  133.0 19.5 %copy-start.15 = (f32[256,256]{0,1:T(8,128)S(1)}, f32[256,256]{0,1:T(8,128)}, u32[]{:S(2)}) copy-start(f32[256,256]{0,1:T(8,128)} %get-tuple-element.158) | copy-start | bytes 786436
  133.0 19.5 %copy-start.16 = (f32[256,256]{0,1:T(8,128)S(1)}, f32[256,256]{0,1:T(8,128)}, u32[]{:S(2)}) copy-start(f32[256,256]{0,1:T(8,128)} %get-tuple-element.159) | copy-start | bytes 786436
  133.0 19.5 %copy-start.17 = (f32[256,256]{0,1:T(8,128)S(1)}, f32[256,256]{0,1:T(8,128)}, u32[]{:S(2)}) copy-start(f32[256,256]{0,1:T(8,128)} %get-tuple-element.160) | copy-start | bytes 786436
  133.0 19.5 %copy-start.18 = (f32[256,256]{0,1:T(8,128)S(1)}, f32[256,256]{0,1:T(8,128)}, u32[]{:S(2)}) copy-start(f32[256,256]{0,1:T(8,128)} %get-tuple-element.161) | copy-start | bytes 786436
  133.0 19.5 %copy-start.19 = (f32[256,256]{0,1:T(8,128)S(1)}, f32[256,256]{0,1:T(8,128)}, u32[]{:S(2)}) copy-start(f32[256,256]{0,1:T(8,128)} %get-tuple-element.162) | copy-start | bytes 786436
  133.1 19.5 %copy-start.20 = (f32[256,256]{0,1:T(8,128)S(1)}, f32[256,256]{0,1:T(8,128)}, u32[]{:S(2)}) copy-start(f32[256,256]{0,1:T(8,128)} %get-tuple-element.163) | copy-start | bytes 786436
  133.1 19.5 %copy-start.21 = (f32[256,256]{0,1:T(8,128)S(1)}, f32[256,256]{0,1:T(8,128)}, u32[]{:S(2)}) copy-start(f32[256,256]{0,1:T(8,128)} %get-tuple-element.36) | copy-start | bytes 786436
  156.8 4.7 %copy-start.24 = (bf16[256,256]{1,0:T(8,128)(2,1)S(1)}, bf16[256,256]{1,0:T(8,128)(2,1)}, u32[]{:S(2)}) copy-start(bf16[256,256]{1,0:T(8,128)(2,1)} %param.6) | copy-start | bytes 393220
  156.8 21.0 %copy-start.11 = (bf16[256,256]{0,1:T(8,128)(2,1)S(1)}, bf16[256,256]{0,1:T(8,128)(2,1)}, u32[]{:S(2)}) copy-start(bf16[256,256]{0,1:T(8,128)(2,1)} %copy-done.10) | copy-start | bytes 393220
  156.8 21.0 %copy-start.42 = (f32[256]{0:T(256)S(1)}, f32[256]{0:T(256)}, u32[]{:S(2)}) copy-start(f32[256]{0:T(256)} %param.9) | copy-start | bytes 3076
  157.9 19.6 %all-to-all-start.2 = ((f32[2,256,256]{1,0,2:T(2,128)}), f32[2,256,256]{1,0,2:T(2,128)S(1)}, u32[]{:S(2)}, u32[]{:S(2)}) async-start(f32[2,256,256]{1,0,2:T(2,128)} %copy.30), calls=%async_computation.2 | async-start | bytes 1048576 | tf_op jit(solution)/shard_map/all_to_all | solution.py:101
  161.5 95.6 %reduce-scatter.2.cloned.1.call-start = ((), (), s32[]{:S(2)}) async-start(), calls=%async_computation.5 | async-start | bytes 2228224 | tf_op jit(solution)/shard_map/reduce_scatter | solution.py:106
  (23 other events, 75.4 us)
Sparse Core Ops, SparseCore 0:
  10.4 54.6 all-gather.1
  180.2 76.7 reduce-scatter.1
where the time goes:
time: 266 us; the launch traced here: 264 us
  waiting for transfers between devices  130 us (49%)
  other arithmetic  54.5 us (20%)
  local copies, waits for them, and re-layouts  28.6 us (11%)
  starting transfers between devices  19.3 us (7%)
  matrix products  17.2 us (6%)
  between operations  14.7 us (6%)
    reduce_scatter x1, waiting for transfers between devices, body(): lax.psum_scatter(partial_out.astype(jnp.bfloat16), 'ch', scatter_dimensio...  76.1 us
    all_gather x1, waiting for transfers between devices, body(): lax.all_gather(cotangent, 'ch', axis=1, tiled=True)  29.8 us
    unnamed x106, local copies, waits for them, and re-layouts  22.3 us
    reduce_sum x16, other arithmetic, body(): lag_terms.append(term.reshape(term.shape[0], ctx_count, width).sum(axis=1))  20.4 us
    sub x11, other arithmetic, spec_product(): real_part = first_real * second_real - others * first_imag * second_imag  18 us
    all_to_all x1, waiting for transfers between devices, body(): lax.all_to_all(jnp.stack([convolved_t, filter_grad_t]), 'ctx', 2, 2, tile...  15.8 us
    all_to_all x1, starting transfers between devices, body(): pair_t = lax.all_to_all(pair, 'ctx', 2, 2, tiled=True)  8.57 us
    concatenate x9, other arithmetic, conj_product(): return jnp.concatenate([real_part, imag_part], axis=-2)  8.04 us
  transfers between devices with their start and end apart: 5, of which 5 were waited for; matrix products, arithmetic and copies ran while one was open for 9% of the time, Pallas kernels for 0%

commit v1 on v0

--- a/solution.py
+++ b/solution.py
@@ -1,3 +1,4 @@
+import functools
 import math
 import jax
 import jax.numpy as jnp
@@ -5,6 +6,17 @@
 from jax.sharding import PartitionSpec as P
 
 exact_prec = lax.Precision.HIGHEST
+
+
+def replace_slot(xs, where_dim, dimension_no):
+    spare = lax.all_to_all(
+        jnp.stack(jnp.split(xs, lax.axis_size("ctx"), axis=where_dim)), "ctx", 0, 0
+    )
+    placed = jnp.concatenate(spare, dimension_no)
+    return placed
+
+
+replace_patches = functools.partial(replace_slot, where_dim=1, dimension_no=1)
 
 
 def spectral_tables(block_len):
@@ -81,7 +93,7 @@
     )
     gate_wide = gating.astype(jnp.float32)
     grad_mixed = upstream * gate_wide
-    grad_t = lax.all_to_all(grad_mixed, "ctx", 1, 1, tiled=True)
+    grad_t = replace_patches(grad_mixed)
     low_spec = transform(first_half, signal_t)
     high_spec = transform(second_half, signal_t)
     seg_spec = high_spec + shift_blocks(low_spec, 1, width)

time: 266 us -> 275 us (1.034)
  local copies, waits for them, and re-layouts: 28.6 us -> 38.3 us
    unnamed x106 -> x121, local copies, waits for them, and re-layouts: 22.3 us -> 31.4 us
  transfers between devices with their start and end apart: 5 -> 5, of which waited for: 5 -> 5; matrix products, arithmetic and copies ran while one was open for 9% -> 8% of each run, Pallas kernels for 0% -> 0%
where the time goes in v1:
time: 275 us; the launch traced here: 273 us
  waiting for transfers between devices  129 us (47%)
  other arithmetic  54.5 us (20%)
  local copies, waits for them, and re-layouts  38.3 us (14%)
  starting transfers between devices  19.3 us (7%)
  matrix products  16.5 us (6%)
  between operations  14.7 us (5%)
    reduce_scatter x1, waiting for transfers between devices, body(): lax.psum_scatter(partial_out.astype(jnp.bfloat16), 'ch', scatter_dimensio...  75.9 us
    unnamed x121, local copies, waits for them, and re-layouts  31.4 us
    all_gather x1, waiting for transfers between devices, body(): lax.all_gather(cotangent, 'ch', axis=1, tiled=True)  29.8 us
    reduce_sum x16, other arithmetic, body(): lag_terms.append(term.reshape(term.shape[0], ctx_count, width).sum(axis=1))  20.4 us
    sub x11, other arithmetic, spec_product(): real_part = first_real * second_real - others * first_imag * second_imag  18 us
    all_to_all x1, waiting for transfers between devices, body(): lax.all_to_all(jnp.stack([convolved_t, filter_grad_t]), 'ctx', 2, 2, tile...  15.8 us
    all_to_all x1, starting transfers between devices, body(): pair_t = lax.all_to_all(pair, 'ctx', 2, 2, tiled=True)  8.57 us
    concatenate x9, other arithmetic, conj_product(): return jnp.concatenate([real_part, imag_part], axis=-2)  8.04 us
  transfers between devices with their start and end apart: 5, of which 5 were waited for; matrix products, arithmetic and copies ran while one was open for 8% of the time, Pallas kernels for 0%

profile of v1, /device:TPU:2, one launch (start us, length us, event | category | flops | bytes accessed | tf_op | source)
XLA Modules:
  0.0 272.7 jit_solution(9645363618873182372)
XLA Ops:
  9.8 8.6 %all-to-all-start = ((bf16[2,256,256]{1,0,2:T(2,128)(2,1)}), bf16[2,256,256]{1,0,2:T(2,128)(2,1)S(1)}, u32[]{:S(2)}, u32[]{:S(2)}) async-start(bf16[2,256,256]{1,0,2:T(2,128)(2,1)} %copy.25), calls=%async_computation | async-start | bytes 524288 | tf_op jit(solution)/shard_map/all_to_all | solution.py:86
  19.4 1.9 fusion.170
  21.3 2.0 multiply_multiply_fusion
  23.3 2.0 select_multiply_fusion
  26.5 3.0 %all-to-all-done = bf16[2,256,256]{1,0,2:T(2,128)(2,1)S(1)} async-done(((bf16[2,256,256]{1,0,2:T(2,128)(2,1)}), bf16[2,256,256]{1,0,2:T(2,128)(2,1)S(1)}, u32[]{:S(2)}, u32[]{:S(2)}) %all-to-all-start) | async-done | bytes 262176 | tf_op jit(solution)/shard_map/all_to_all | solution.py:86
  35.3 29.8 %all-gather.2.cloned.1.call-done = bf16[256,4096]{1,0:T(8,128)(2,1)} async-done(((bf16[256,256]{1,0:T(8,128)(2,1)}), bf16[256,4096]{1,0:T(8,128)(2,1)}) %all-gather.2.cloned.1.call-update) | async-done | bytes 2097168 | tf_op jit(solution)/shard_map/all_gather | solution.py:89
  65.1 2.3 convolution_multiply_fusion
  77.1 7.1 %all-to-all-start.1 = ((f32[16,256,16]{1,2,0:T(8,128)}), f32[16,256,16]{1,2,0:T(8,128)S(1)}, u32[]{:S(2)}, u32[]{:S(2)}) async-start(f32[16,256,16]{1,2,0:T(8,128)} %constant_dynamic-update-slice_fusion), calls=%async_computation.1 | async-start | bytes 524288 | tf_op jit(solution)/shard_map/all_to_all | solution.py:12
  91.3 4.2 %all-to-all-done.1 = f32[16,256,16]{1,2,0:T(8,128)S(1)} async-done(((f32[16,256,16]{1,2,0:T(8,128)}), f32[16,256,16]{1,2,0:T(8,128)S(1)}, u32[]{:S(2)}, u32[]{:S(2)}) %all-to-all-start.1) | async-done | bytes 262176 | tf_op jit(solution)/shard_map/all_to_all | solution.py:12
  95.4 1.7 fusion.171
  97.1 1.7 fusion.72
  99.6 2.7 fusion.76
  103.4 1.7 reduce_sum.145
  105.1 1.7 reduce_sum.159
  108.7 1.7 reduce_sum.147
  111.0 2.0 fusion.88
  114.2 1.7 reduce_sum.148
  119.0 1.7 reduce_sum.146
  121.3 2.1 fusion.92
  124.4 1.7 reduce_sum.149
  126.7 1.9 fusion.132
  129.5 1.7 reduce_sum.152
  133.1 1.7 reduce_sum.151
  135.5 2.1 fusion.96
  138.6 1.7 reduce_sum.150
  140.4 1.7 reduce_sum.154
  159.5 2.0 convolution_bitcast_fusion
  161.6 4.2 %convolution_bitcast_fusion.1 = f32[1,256,256]{2,1,0:T(8,128)S(1)} fusion(f32[512,512]{0,1:T(8,128)S(1)} %copy-done.4, f32[256,256]{0,1:T(8,128)} %get-tuple-element.37, f32[256,256]{0,1:T(8,128)S(1)} %copy-done.21, f32[256,256]{0,1:T(8,128)} %get-tuple-element.57, f32[256,256]{0,1:T(8,128)} %get-tuple-element.56, f32[256,256]{0,1:T(8,128)} %get-tuple-element.97, ...), kind=kOutput, calls=%fused_computation.3 | convolution fusion | flops 406716416 | bytes 9175040 | tf_op jit(solution)/shard_map/dot_general | solution.py:111
  166.9 3.6 %all-to-all-start.2 = ((f32[2,256,256]{1,0,2:T(2,128)}), f32[2,256,256]{1,0,2:T(2,128)S(1)}, u32[]{:S(2)}, u32[]{:S(2)}) async-start(f32[2,256,256]{1,0,2:T(2,128)} %copy.30), calls=%async_computation.2 | async-start | bytes 1048576 | tf_op jit(solution)/shard_map/all_to_all | solution.py:113
  170.6 15.8 %all-to-all-done.2 = f32[2,256,256]{1,0,2:T(2,128)S(1)} async-done(((f32[2,256,256]{1,0,2:T(2,128)}), f32[2,256,256]{1,0,2:T(2,128)S(1)}, u32[]{:S(2)}, u32[]{:S(2)}) %all-to-all-start.2) | async-done | bytes 524320 | tf_op jit(solution)/shard_map/all_to_all | solution.py:113
  186.9 2.2 convolution_convert_fusion
  189.9 75.9 %reduce-scatter.2.cloned.1.call-done = bf16[256,256]{1,0:T(8,128)(2,1)} async-done(((bf16[256,4096]{1,0:T(8,128)(2,1)}), bf16[256,256]{1,0:T(8,128)(2,1)}) %reduce-scatter.2.cloned.1.call-update) | async-done | bytes 131088 | tf_op jit(solution)/shard_map/reduce_scatter | solution.py:118
  (186 shorter events, 62.5 us)
Async XLA Ops:
  7.2 57.9 %copy-start = (bf16[256,4096]{1,0:T(8,128)(2,1)S(1)}, bf16[256,4096]{1,0:T(8,128)(2,1)}, u32[]{:S(2)}) copy-start(bf16[256,4096]{1,0:T(8,128)(2,1)} %param.10) | copy-start | bytes 6291460
  7.2 57.9 %all-gather.2.cloned.1.call-start = ((), (), s32[]{:S(2)}) async-start(), calls=%async_computation.4 | async-start | bytes 2228224 | tf_op jit(solution)/shard_map/all_gather | solution.py:89
  9.8 19.7 %all-to-all-start = ((bf16[2,256,256]{1,0,2:T(2,128)(2,1)}), bf16[2,256,256]{1,0,2:T(2,128)(2,1)S(1)}, u32[]{:S(2)}, u32[]{:S(2)}) async-start(bf16[2,256,256]{1,0,2:T(2,128)(2,1)} %copy.25), calls=%async_computation | async-start | bytes 524288 | tf_op jit(solution)/shard_map/all_to_all | solution.py:86
  19.4 45.7 %copy-start.10 = (bf16[256,256]{0,1:T(8,128)(2,1)}, bf16[256,256]{0,1:T(8,128)(2,1)S(1)}, u32[]{:S(2)}) copy-start(bf16[256,256]{0,1:T(8,128)(2,1)S(1)} %copy.24) | copy-start | bytes 393220
  21.3 62.9 %copy-start.2 = (f32[256,512]{1,0:T(8,128)}, f32[256,512]{1,0:T(8,128)S(1)}, u32[]{:S(2)}) copy-start(f32[256,512]{1,0:T(8,128)S(1)} %fusion.170) | copy-start | bytes 1572868
  25.4 8.7 %copy-start.3 = (f32[256,512]{1,0:T(8,128)}, f32[256,512]{1,0:T(8,128)S(1)}, u32[]{:S(2)}) copy-start(f32[256,512]{1,0:T(8,128)S(1)} %get-tuple-element.153) | copy-start | bytes 1572868
  77.1 18.3 %all-to-all-start.1 = ((f32[16,256,16]{1,2,0:T(8,128)}), f32[16,256,16]{1,2,0:T(8,128)S(1)}, u32[]{:S(2)}, u32[]{:S(2)}) async-start(f32[16,256,16]{1,2,0:T(8,128)} %constant_dynamic-update-slice_fusion), calls=%async_computation.1 | async-start | bytes 524288 | tf_op jit(solution)/shard_map/all_to_all | solution.py:12
  85.9 11.2 %copy-start.1 = (f32[512,256]{0,1:T(8,128)}, f32[512,256]{0,1:T(8,128)S(1)}, u32[]{:S(2)}) copy-start(f32[512,256]{0,1:T(8,128)S(1)} %convolution_add_fusion) | copy-start | bytes 1572868
  85.9 13.7 %copy-start.25 = (f32[512,16]{0,1:T(8,128)}, f32[512,16]{0,1:T(8,128)S(1)}, u32[]{:S(2)}) copy-start(f32[512,16]{0,1:T(8,128)S(1)} %slice.604) | copy-start | bytes 98308
  102.2 4.5 %slice-start.5 = ((f32[512,256]{0,1:T(8,128)}), f32[512,208]{0,1:T(8,128)S(1)}, s32[]{:S(2)}) async-start(f32[512,256]{0,1:T(8,128)} %copy-done.1), calls=%async_computation.11 | async-start | bytes 851968 | tf_op jit(solution)/shard_map/slice | solution.py:75
  102.2 4.5 %copy-start.38 = (f32[256,16]{0,1:T(8,128)S(1)}, f32[256,16]{0,1:T(8,128)}, u32[]{:S(2)}) copy-start(f32[256,16]{0,1:T(8,128)} %get-tuple-element.84) | copy-start | bytes 49156
  102.3 4.5 %copy-start.39 = (f32[256,16]{0,1:T(8,128)S(1)}, f32[256,16]{0,1:T(8,128)}, u32[]{:S(2)}) copy-start(f32[256,16]{0,1:T(8,128)} %get-tuple-element.85) | copy-start | bytes 49156
  126.7 4.5 %copy-start.31 = (f32[256,16]{0,1:T(8,128)S(1)}, f32[256,16]{0,1:T(8,128)}, u32[]{:S(2)}) copy-start(f32[256,16]{0,1:T(8,128)} %get-tuple-element.76) | copy-start | bytes 49156
  126.7 4.5 %copy-start.32 = (f32[256,16]{0,1:T(8,128)S(1)}, f32[256,16]{0,1:T(8,128)}, u32[]{:S(2)}) copy-start(f32[256,16]{0,1:T(8,128)} %get-tuple-element.77) | copy-start | bytes 49156
  137.5 4.5 %copy-start.29 = (f32[512,16]{0,1:T(8,128)S(1)}, f32[512,16]{0,1:T(8,128)}, u32[]{:S(2)}) copy-start(f32[512,16]{0,1:T(8,128)} %reduce_sum.145) | copy-start | bytes 98308
  137.5 19.4 %copy-start.28 = (f32[512,16]{0,1:T(8,128)S(1)}, f32[512,16]{0,1:T(8,128)}, u32[]{:S(2)}) copy-start(f32[512,16]{0,1:T(8,128)} %reduce_sum.157) | copy-start | bytes 98308
  137.5 21.4 %copy-start.27 = (f32[512,16]{0,1:T(8,128)S(1)}, f32[512,16]{0,1:T(8,128)}, u32[]{:S(2)}) copy-start(f32[512,16]{0,1:T(8,128)} %reduce_sum.159) | copy-start | bytes 98308
  137.5 22.0 %copy-start.4 = (f32[512,512]{0,1:T(8,128)S(1)}, f32[512,512]{0,1:T(8,128)}, u32[]{:S(2)}) copy-start(f32[512,512]{0,1:T(8,128)} %maximum_bitcast_fusion) | copy-start | bytes 3145732
  138.6 22.9 %copy-start.13 = (f32[256,256]{0,1:T(8,128)S(1)}, f32[256,256]{0,1:T(8,128)}, u32[]{:S(2)}) copy-start(f32[256,256]{0,1:T(8,128)} %get-tuple-element.148) | copy-start | bytes 786436
  142.0 19.5 %copy-start.14 = (f32[256,256]{0,1:T(8,128)S(1)}, f32[256,256]{0,1:T(8,128)}, u32[]{:S(2)}) copy-start(f32[256,256]{0,1:T(8,128)} %get-tuple-element.149) | copy-start | bytes 786436
  142.0 19.5 %copy-start.15 = (f32[256,256]{0,1:T(8,128)S(1)}, f32[256,256]{0,1:T(8,128)}, u32[]{:S(2)}) copy-start(f32[256,256]{0,1:T(8,128)} %get-tuple-element.158) | copy-start | bytes 786436
  142.0 19.5 %copy-start.16 = (f32[256,256]{0,1:T(8,128)S(1)}, f32[256,256]{0,1:T(8,128)}, u32[]{:S(2)}) copy-start(f32[256,256]{0,1:T(8,128)} %get-tuple-element.159) | copy-start | bytes 786436
  142.0 19.5 %copy-start.17 = (f32[256,256]{0,1:T(8,128)S(1)}, f32[256,256]{0,1:T(8,128)}, u32[]{:S(2)}) copy-start(f32[256,256]{0,1:T(8,128)} %get-tuple-element.160) | copy-start | bytes 786436
  142.1 19.5 %copy-start.18 = (f32[256,256]{0,1:T(8,128)S(1)}, f32[256,256]{0,1:T(8,128)}, u32[]{:S(2)}) copy-start(f32[256,256]{0,1:T(8,128)} %get-tuple-element.161) | copy-start | bytes 786436
  142.1 19.5 %copy-start.19 = (f32[256,256]{0,1:T(8,128)S(1)}, f32[256,256]{0,1:T(8,128)}, u32[]{:S(2)}) copy-start(f32[256,256]{0,1:T(8,128)} %get-tuple-element.162) | copy-start | bytes 786436
  142.1 19.5 %copy-start.20 = (f32[256,256]{0,1:T(8,128)S(1)}, f32[256,256]{0,1:T(8,128)}, u32[]{:S(2)}) copy-start(f32[256,256]{0,1:T(8,128)} %get-tuple-element.163) | copy-start | bytes 786436
  142.1 19.5 %copy-start.21 = (f32[256,256]{0,1:T(8,128)S(1)}, f32[256,256]{0,1:T(8,128)}, u32[]{:S(2)}) copy-start(f32[256,256]{0,1:T(8,128)} %get-tuple-element.36) | copy-start | bytes 786436
  165.8 4.7 %copy-start.24 = (bf16[256,256]{1,0:T(8,128)(2,1)S(1)}, bf16[256,256]{1,0:T(8,128)(2,1)}, u32[]{:S(2)}) copy-start(bf16[256,256]{1,0:T(8,128)(2,1)} %param.6) | copy-start | bytes 393220
  165.8 21.0 %copy-start.11 = (bf16[256,256]{0,1:T(8,128)(2,1)S(1)}, bf16[256,256]{0,1:T(8,128)(2,1)}, u32[]{:S(2)}) copy-start(bf16[256,256]{0,1:T(8,128)(2,1)} %copy-done.10) | copy-start | bytes 393220
  165.9 21.0 %copy-start.42 = (f32[256]{0:T(256)S(1)}, f32[256]{0:T(256)}, u32[]{:S(2)}) copy-start(f32[256]{0:T(256)} %param.9) | copy-start | bytes 3076
  166.9 19.6 %all-to-all-start.2 = ((f32[2,256,256]{1,0,2:T(2,128)}), f32[2,256,256]{1,0,2:T(2,128)S(1)}, u32[]{:S(2)}, u32[]{:S(2)}) async-start(f32[2,256,256]{1,0,2:T(2,128)} %copy.30), calls=%async_computation.2 | async-start | bytes 1048576 | tf_op jit(solution)/shard_map/all_to_all | solution.py:113
  170.5 95.4 %reduce-scatter.2.cloned.1.call-start = ((), (), s32[]{:S(2)}) async-start(), calls=%async_computation.5 | async-start | bytes 2228224 | tf_op jit(solution)/shard_map/reduce_scatter | solution.py:118
  (23 other events, 75.4 us)
Sparse Core Ops, SparseCore 0:
  10.4 54.6 all-gather.1
  189.2 76.5 reduce-scatter.1
